TPU v7x, 32 devices: a whole 2x2x4 slice. The times are simulated.
32 devices in a mesh: seq: 8 (over y, x, core), head: 4 (over z).
Axes of the slice: x: 2, y: 2, z: 4, core: 2. Of those that a mesh axis runs over, the one named last changes fastest.
Arguments:
- queries: bfloat16 [4096, 4096], P('seq', 'head'), may hold values from -6 to 6
- keys: bfloat16 [4096, 4096], P('seq', 'head'), may hold values from -6 to 6
- values: bfloat16 [4096, 4096], P('seq', 'head'), may hold values from -48 to 48
- gate_logits: bfloat16 [4096, 4096], P('seq', 'head'), may hold values from -8 to 8
- out_weight: bfloat16 [4096, 6144], P('head'), may hold values from -0.125 to 0.125
Outputs:
- layer_out: bfloat16 [4096, 6144], P('seq', 'head')
All inputs are finite; a program needn't handle non-finite values.
Results may differ from a plain program's by a relative error of at most 0.02.
Values may be sent and summed in bfloat16 or wider, within the bound.
No kernel may reach another device: no remote copies, remote signals or barrier semaphores. Data moves between devices by JAX's collectives and lax.ppermute only.
A program may use at most 64 MiB of HBM per device.

v0:
```python
import jax
import jax.numpy as jnp
from jax import lax
from jax.sharding import PartitionSpec as P

HEADS = 32
HEAD_DIM = 128


def activate(raw_input):
    return jax.nn.silu(raw_input.astype(jnp.float32)).astype(jnp.bfloat16)


def body(queries, keys, values, gate_logits, out_weight):
    tokens_here = queries.shape[0]
    feature_count = queries.shape[1]
    heads_here = feature_count // HEAD_DIM
    block_rows = min(512, tokens_here)
    block_count = tokens_here // block_rows
    shape_blocks = (block_count, block_rows, heads_here, HEAD_DIM)
    active_q = activate(queries).reshape(shape_blocks)
    active_k = activate(keys).reshape(shape_blocks)
    active_v = activate(values).reshape(shape_blocks)
    block_states = jnp.einsum(
        "nshd,nshe->nhde", active_k, active_v, preferred_element_type=jnp.float32
    )
    span_total = jnp.sum(block_states, axis=0)
    earlier_local = jnp.cumsum(block_states, axis=0) - block_states
    my_index = lax.axis_index("seq")
    shards = lax.all_gather(
        span_total[None].astype(jnp.bfloat16), "seq", axis=0, tiled=True
    ).astype(jnp.float32)
    positions = jnp.arange(shards.shape[0], dtype=jnp.int32)
    weights = (positions < my_index).astype(jnp.float32)
    prefix = jnp.zeros_like(span_total) + jnp.sum(shards * weights[:, None, None, None], axis=0)
    before = (prefix[None] + earlier_local).astype(jnp.bfloat16)
    causal_mask = jnp.tril(jnp.ones((block_rows, block_rows), jnp.float32))
    scores = jnp.einsum("nthd,nshd->nhts", active_q, active_k, preferred_element_type=jnp.float32)
    scores = (scores * causal_mask).astype(jnp.bfloat16)
    within_block = jnp.einsum(
        "nhts,nshd->nthd", scores, active_v, preferred_element_type=jnp.float32
    )
    from_state = jnp.einsum("nthd,nhde->nthe", active_q, before, preferred_element_type=jnp.float32)
    attended = (within_block + from_state).reshape(tokens_here, feature_count)
    square_sums = lax.psum(jnp.sum(attended * attended, axis=-1), "head")
    scaling = lax.rsqrt(square_sums / (HEADS * HEAD_DIM) + 1e-06)
    gate = jax.nn.sigmoid(gate_logits.astype(jnp.float32))
    normed = (attended * scaling[:, None] * gate).astype(jnp.bfloat16)
    reduced = lax.psum_scatter(
        lax.dot_general(
            out_weight, normed, (((0,), (1,)), ((), ())), preferred_element_type=jnp.float32
        ).astype(jnp.bfloat16),
        "head",
        scatter_dimension=0,
        tiled=True,
    ).astype(jnp.float32)
    return reduced.T.astype(jnp.bfloat16)


def solution(mesh):
    return jax.shard_map(
        body,
        mesh=mesh,
        in_specs=(
            P("seq", "head"),
            P("seq", "head"),
            P("seq", "head"),
            P("seq", "head"),
            P("head", None),
        ),
        out_specs=P("seq", "head"),
        check_vma=False,
    )
```

profile of v0, /device:TPU:0, one launch (start us, length us, event | category | flops | bytes accessed | tf_op | source)
XLA Modules:
  0.0 192.8 jit_solution(12036253391915671986)
XLA Ops:
  6.5 0.0 copy-start
  6.5 0.0 all-gather.3.cloned.1.call-start
  6.5 1.9 fusion.17
  8.5 0.5 copy.19
  9.0 0.0 copy-done
  9.0 1.8 fusion.38
  10.8 0.0 copy-start.1
  10.8 0.0 copy-start.2
  10.8 0.0 all-gather.3.cloned.1.call-update
  10.8 0.0 reduce-scatter.2.cloned.1.call-start
  10.9 1.1 fusion.31
  12.0 29.5 %all-gather.3.cloned.1.call-done = bf16[64,128,128]{2,1,0:T(8,128)(2,1)} async-done(((bf16[8,128,128]{2,1,0:T(8,128)(2,1)}), bf16[64,128,128]{2,1,0:T(8,128)(2,1)}) %all-gather.3.cloned.1.call-update) | async-done | bytes 2097168 | tf_op jit(solution)/shard_map/all_gather | solution.py:30
  41.5 2.1 %fusion.2 = f32[8,128,128]{2,1,0:T(8,128)S(1)} fusion(bf16[8,8,128,128]{3,2,1,0:T(8,128)(2,1)} %bitcast.47, f32[8]{0:T(128)S(1)} %compare_convert_fusion), kind=kLoop, calls=%fused_computation.5 | loop fusion | flops 3014656 | bytes 2621472 | tf_op jit(solution)/shard_map/reduce_sum | solution.py:35
  43.6 0.0 copy-done.1
  43.6 0.0 copy-done.2
  43.6 2.2 %fusion.24 = f32[8,128,512]{2,1,0:T(8,128)} fusion(f32[8,128,128]{2,1,0:T(8,128)S(1)} %fusion.2, f32[8,128,128]{2,1,0:T(8,128)S(1)} %copy-done.2, bf16[512,1024]{1,0:T(8,128)(2,1)S(1)} %copy-done.1), kind=kOutput, calls=%fused_computation.33 | convolution fusion | flops 137756672 | bytes 4194304 | tf_op jit(solution)/shard_map/nthd,nhde->nthe/dot_general | solution.py:43
  45.8 5.3 %fusion.18 = (f32[512]{0:T(512)S(1)}, f32[8,128,512]{2,1,0:T(8,128)S(1)}) fusion(f32[8,128,512]{2,1,0:T(8,128)} %fusion.24, f32[512,512]{1,0:T(8,128)} %fusion.31, bf16[512,8,128]{0,2,1:T(8,128)(2,1)S(1)} %bitcast.50, bf16[512,1024]{1,0:T(8,128)(2,1)} %param.7, bf16[512,1024]{1,0:T(8,128)(2,1)} %param.5), kind=kOutput, calls=%fused_computation.27 | convolution fusion | flops 1085799936 | bytes 8390656 | tf_op jit(solution)/shard_map/nhts,nshd->nthd/dot_general | solution.py:40
  51.1 11.7 %psum.7 = f32[512]{0:T(512)S(1)} all-reduce(f32[512]{0:T(512)S(1)} %get-tuple-element.7), channel_id=1, replica_groups=mesh['seq'=8,'head'=4] {'head'}, use_global_device_ids=true, to_apply=%region_2.3 | all-reduce | flops 512 | bytes 4096 | tf_op jit(solution)/shard_map/psum | solution.py:45
  62.8 1.8 copy.17
  64.6 13.1 %fusion = bf16[6144,512]{0,1:T(8,128)(2,1)} fusion(bf16[1024,6144]{1,0:T(8,128)(2,1)} %param.9, bf16[512,1024]{1,0:T(8,128)(2,1)} %param.8, f32[512,1024]{1,0:T(8,128)} %copy.17, f32[512]{0:T(512)S(1)} %add_rsqrt_fusion), kind=kOutput, calls=%fused_computation.2 | convolution fusion | flops 6449266688 | bytes 22022144 | tf_op jit(solution)/shard_map/dot_general | solution.py:50
  77.8 0.0 reduce-scatter.2.cloned.1.call-update
  77.8 108.2 %reduce-scatter.2.cloned.1.call-done = bf16[1536,512]{0,1:T(8,128)(2,1)} async-done(((bf16[6144,512]{0,1:T(8,128)(2,1)}), bf16[1536,512]{0,1:T(8,128)(2,1)}) %reduce-scatter.2.cloned.1.call-update) | async-done | bytes 1572880 | tf_op jit(solution)/shard_map/reduce_scatter | solution.py:49
  (2 shorter events, 0.0 us)
Async XLA Ops:
  6.5 2.5 %copy-start = (bf16[512,1024]{1,0:T(8,128)(2,1)S(1)}, bf16[512,1024]{1,0:T(8,128)(2,1)}, u32[]{:S(2)}) copy-start(bf16[512,1024]{1,0:T(8,128)(2,1)} %param.7) | copy-start | bytes 3145732
  6.5 34.9 %all-gather.3.cloned.1.call-start = ((), (), s32[]{:S(2)}) async-start(), calls=%async_computation.2 | async-start | bytes 2359296 | tf_op jit(solution)/shard_map/all_gather | solution.py:30
  10.8 32.8 %copy-start.1 = (bf16[512,1024]{1,0:T(8,128)(2,1)S(1)}, bf16[512,1024]{1,0:T(8,128)(2,1)}, u32[]{:S(2)}) copy-start(bf16[512,1024]{1,0:T(8,128)(2,1)} %param.5) | copy-start | bytes 3145732
  10.8 32.8 %copy-start.2 = (f32[8,128,128]{2,1,0:T(8,128)S(1)}, f32[8,128,128]{2,1,0:T(8,128)}, u32[]{:S(2)}) copy-start(f32[8,128,128]{2,1,0:T(8,128)} %get-tuple-element.6) | copy-start | bytes 1572868
  10.8 175.1 %reduce-scatter.2.cloned.1.call-start = ((), (), s32[]{:S(2)}) async-start(), calls=%async_computation.1 | async-start | bytes 7864320 | tf_op jit(solution)/shard_map/reduce_scatter | solution.py:49
Sparse Core Ops, SparseCore 0:
  10.9 30.4 all-gather.2
  77.9 107.9 reduce-scatter.1
where the time goes:
time: 193 us
  waiting for transfers between devices  138 us (72%)
  matrix products  22.3 us (12%)
  between operations  13.5 us (7%)
  blocking collectives  11.7 us (6%)
  other arithmetic  5.15 us (3%)
  local copies, waits for them, and re-layouts  2.39 us (1%)
    reduce_scatter x1, waiting for transfers between devices, body(): lax.psum_scatter(lax.dot_general(out_weight, normed, (((0,), (1,)), ((),...  108 us
    all_gather x1, waiting for transfers between devices, body(): lax.all_gather(span_total[None].astype(jnp.bfloat16), 'seq', axis=0, tile...  29.5 us
    dot_general x1, matrix products, body(): lax.dot_general(out_weight, normed, (((0,), (1,)), ((), ())), preferred_e...  13.1 us
    psum x1, blocking collectives, body(): square_sums = lax.psum(jnp.sum(attended * attended, axis=-1), 'head')  11.7 us
    dot_general x1, matrix products, body(): jnp.einsum('nhts,nshd->nthd', scores, active_v, preferred_element_type=jn...  5.26 us
  transfers between devices with their start and end apart: 2, of which 2 were waited for; matrix products, arithmetic and copies ran while one was open for 1% of the time, Pallas kernels for 0%

commit v1 on v0

--- a/solution.py
+++ b/solution.py
@@ -5,6 +5,19 @@
 
 HEADS = 32
 HEAD_DIM = 128
+
+
+def collect(shard, axis, dim):
+    ways = lax.axis_size(axis)
+    up = [(d, (d + 1) % ways) for d in range(ways)]
+    down = [(d, (d - 1) % ways) for d in range(ways)]
+    earlier, later = ([shard], [shard])
+    for _ in range(ways // 2):
+        earlier.append(lax.ppermute(earlier[-1], axis, up))
+    for _ in range((ways - 1) // 2):
+        later.append(lax.ppermute(later[-1], axis, down))
+    line = jnp.concatenate([*earlier[::-1], *later[1:]], axis=dim)
+    return jnp.roll(line, (lax.axis_index(axis) - ways // 2) * shard.shape[dim], axis=dim)
 
 
 def activate(raw_input):
@@ -27,9 +40,7 @@
     span_total = jnp.sum(block_states, axis=0)
     earlier_local = jnp.cumsum(block_states, axis=0) - block_states
     my_index = lax.axis_index("seq")
-    shards = lax.all_gather(
-        span_total[None].astype(jnp.bfloat16), "seq", axis=0, tiled=True
-    ).astype(jnp.float32)
+    shards = collect(span_total[None].astype(jnp.bfloat16), "seq", 0).astype(jnp.float32)
     positions = jnp.arange(shards.shape[0], dtype=jnp.int32)
     weights = (positions < my_index).astype(jnp.float32)
     prefix = jnp.zeros_like(span_total) + jnp.sum(shards * weights[:, None, None, None], axis=0)

time: 193 us -> 197 us (1.021)
  waiting for transfers between devices: 138 us -> 127 us
  starting transfers between devices: 0.04 us -> 8.58 us
  local copies, waits for them, and re-layouts: 2.39 us -> 8.82 us
  blocking collectives: 11.7 us -> 14.2 us
  other arithmetic: 5.15 us -> 2.67 us
    all_gather x1 -> x0, waiting for transfers between devices: 29.5 us -> none  [body(): lax.all_gather(span_total[None].astype(jnp.bfloat16), 'seq', axis=0, tile...]
    ppermute x0 -> x7, waiting for transfers between devices: none -> 18.7 us  [the longest x4 17.8 us: collect(): earlier.append(lax.ppermute(earlier[-1], axis, up))]
    ppermute x0 -> x7, starting transfers between devices: none -> 8.58 us  [the longest x3 8.02 us: collect(): later.append(lax.ppermute(later[-1], axis, down))]
    unnamed x6 -> x19, local copies, waits for them, and re-layouts: 0.01 us -> 6.32 us
    psum x1, blocking collectives: 11.7 us -> 14.2 us  [body(): square_sums = lax.psum(jnp.sum(attended * attended, axis=-1), 'head')]
  transfers between devices with their start and end apart: 2 -> 8, of which waited for: 2 -> 5; matrix products, arithmetic and copies ran while one was open for 1% -> 5% of each run, Pallas kernels for 0% -> 0%
where the time goes in v1:
time: 197 us; the launch traced here: 196 us
  waiting for transfers between devices  127 us (64%)
  matrix products  21.1 us (11%)
  blocking collectives  14.2 us (7%)
  between operations  13.6 us (7%)
  local copies, waits for them, and re-layouts  8.82 us (4%)
  starting transfers between devices  8.58 us (4%)
  other arithmetic  2.67 us (1%)
    reduce_scatter x1, waiting for transfers between devices, body(): lax.psum_scatter(lax.dot_general(out_weight, normed, (((0,), (1,)), ((),...  108 us
    ppermute x4, waiting for transfers between devices, collect(): earlier.append(lax.ppermute(earlier[-1], axis, up))  17.8 us
    psum x1, blocking collectives, body(): square_sums = lax.psum(jnp.sum(attended * attended, axis=-1), 'head')  14.2 us
    dot_general x1, matrix products, body(): lax.dot_general(out_weight, normed, (((0,), (1,)), ((), ())), preferred_e...  12.4 us
    ppermute x3, starting transfers between devices, collect(): later.append(lax.ppermute(later[-1], axis, down))  8.02 us
    unnamed x19, local copies, waits for them, and re-layouts  6.32 us
    dot_general x1, matrix products, body(): jnp.einsum('nhts,nshd->nthd', scores, active_v, preferred_element_type=jn...  5.6 us
  transfers between devices with their start and end apart: 8, of which 5 were waited for; matrix products, arithmetic and copies ran while one was open for 5% of the time, Pallas kernels for 0%

profile of v1, /device:TPU:0, one launch (start us, length us, event | category | flops | bytes accessed | tf_op | source)
XLA Modules:
  0.0 196.2 jit_solution(545238483701542012)
XLA Ops:
  6.5 1.9 fusion.16
  8.5 0.5 copy.13
  9.0 0.8 fusion.24
  9.9 0.5 collective-permute-start
  10.5 6.9 %collective-permute-done = bf16[1,8,128,128]{3,2,1,0:T(8,128)(2,1)S(1)} collective-permute-done((bf16[1,8,128,128]{3,2,1,0:T(8,128)(2,1)S(1)}, bf16[1,8,128,128]{3,2,1,0:T(8,128)(2,1)S(1)}, u32[]{:S(2)}, u32[]{:S(2)}) %collective-permute-start) | collective-permute-done | bytes 262176 | tf_op jit(solution)/shard_map/ppermute | solution.py:16
  17.4 0.0 collective-permute-start.1
  17.4 2.6 %collective-permute-start.4 = (bf16[1,8,128,128]{3,2,1,0:T(8,128)(2,1)S(1)}, bf16[1,8,128,128]{3,2,1,0:T(8,128)(2,1)S(1)}, u32[]{:S(2)}, u32[]{:S(2)}) collective-permute-start(bf16[1,8,128,128]{3,2,1,0:T(8,128)(2,1)S(1)} %convert_bitcast_fusion), channel_id=1, source_target_pairs={{0,28},{4,0},{8,4},{12,8},{16,12},{20,16},{24,20},{28,24},{1,29},{... | collective-permute-start | bytes 786440 | tf_op jit(solution)/shard_map/ppermute | solution.py:18
  20.0 5.2 %collective-permute-done.1 = bf16[1,8,128,128]{3,2,1,0:T(8,128)(2,1)S(1)} collective-permute-done((bf16[1,8,128,128]{3,2,1,0:T(8,128)(2,1)S(1)}, bf16[1,8,128,128]{3,2,1,0:T(8,128)(2,1)S(1)}, u32[]{:S(2)}, u32[]{:S(2)}) %collective-permute-start.1) | collective-permute-done | bytes 262176 | tf_op jit(solution)/shard_map/ppermute | solution.py:16
  25.2 0.1 fusion.28
  25.3 2.7 %collective-permute-start.5 = (bf16[1,8,128,128]{3,2,1,0:T(8,128)(2,1)S(1)}, bf16[1,8,128,128]{3,2,1,0:T(8,128)(2,1)}, u32[]{:S(2)}, u32[]{:S(2)}) collective-permute-start(bf16[1,8,128,128]{3,2,1,0:T(8,128)(2,1)S(1)} %collective-permute-done.4), channel_id=1, source_target_pairs={{0,28},{4,0},{8,4},{12,8},{16,12},{20,16},{24,20},{28,24},{1,29},{... | collective-permute-start | bytes 786440 | tf_op jit(solution)/shard_map/ppermute | solution.py:18
  28.0 5.7 %collective-permute-done.2 = bf16[1,8,128,128]{3,2,1,0:T(8,128)(2,1)} collective-permute-done((bf16[1,8,128,128]{3,2,1,0:T(8,128)(2,1)S(1)}, bf16[1,8,128,128]{3,2,1,0:T(8,128)(2,1)}, u32[]{:S(2)}, u32[]{:S(2)}) %collective-permute-start.2) | collective-permute-done | bytes 262176 | tf_op jit(solution)/shard_map/ppermute | solution.py:16
  33.7 0.0 collective-permute-start.3
  33.7 5.6 %fusion.1 = f32[8,128,512]{2,1,0:T(8,128)} fusion(f32[512,512]{1,0:T(8,128)S(1)} %fusion.28, bf16[512,8,128]{0,2,1:T(8,128)(2,1)S(1)} %bitcast.49, bf16[512,1024]{1,0:T(8,128)(2,1)} %param.7, bf16[512,1024]{1,0:T(8,128)(2,1)} %param.5), kind=kOutput, calls=%fused_computation.3 | convolution fusion | flops 1084227584 | bytes 6291456 | tf_op jit(solution)/shard_map/nhts,nshd->nthd/dot_general | solution.py:51
  39.3 0.0 collective-permute-done.5
  39.3 2.7 %collective-permute-start.6 = (bf16[1,8,128,128]{3,2,1,0:T(8,128)(2,1)}, bf16[1,8,128,128]{3,2,1,0:T(8,128)(2,1)S(1)}, u32[]{:S(2)}, u32[]{:S(2)}) collective-permute-start(bf16[1,8,128,128]{3,2,1,0:T(8,128)(2,1)} %collective-permute-done.5), channel_id=1, source_target_pairs={{0,28},{4,0},{8,4},{12,8},{16,12},{20,16},{24,20},{28,24},{1,29},{... | collective-permute-start | bytes 786440 | tf_op jit(solution)/shard_map/ppermute | solution.py:18
  42.0 1.0 constant_dynamic-update-slice_fusion.15
  43.0 1.0 constant_dynamic-update-slice_fusion.14
  44.1 0.1 constant_dynamic-update-slice_fusion.11
  44.2 0.0 copy-start.1
  44.2 1.1 constant_dynamic-update-slice_fusion.9
  45.3 0.9 collective-permute-done.6
  46.3 1.0 constant_dynamic-update-slice_fusion.7
  47.2 1.0 constant_dynamic-update-slice_fusion.6
  48.3 0.1 constant_dynamic-update-slice_fusion.3
  48.4 1.0 constant_dynamic-update-slice_fusion.1
  49.5 0.5 multiply_reduce_fusion
  50.0 2.3 %fusion.17 = (f32[512]{0:T(512)S(1)}, f32[8,128,512]{2,1,0:T(8,128)}) fusion(f32[8,128,512]{2,1,0:T(8,128)S(1)} %copy-done.2, f32[8,128,128]{2,1,0:T(8,128)S(1)} %multiply_reduce_fusion, f32[8,128,128]{2,1,0:T(8,128)S(1)} %fusion.24, bf16[512,1024]{1,0:T(8,128)(2,1)S(1)} %copy-done.1), kind=kOutput, calls=%fused_computation.26 | convolution fusion | flops 139329024 | bytes 6293504 | tf_op jit(solution)/shard_map/nthd,nhde->nthe/dot_general | solution.py:54
  52.2 1.9 copy.11
  54.2 14.2 %psum.7 = f32[512]{0:T(512)S(1)} all-reduce(f32[512]{0:T(512)S(1)} %get-tuple-element.5), channel_id=1, replica_groups=mesh['seq'=8,'head'=4] {'head'}, use_global_device_ids=true, to_apply=%region_2.3 | all-reduce | flops 512 | bytes 4096 | tf_op jit(solution)/shard_map/psum | solution.py:56
  68.4 12.4 %fusion = bf16[6144,512]{0,1:T(8,128)(2,1)} fusion(bf16[1024,6144]{1,0:T(8,128)(2,1)} %param.9, bf16[512,1024]{1,0:T(8,128)(2,1)} %param.8, f32[512,1024]{1,0:T(8,128)S(1)} %copy.11, f32[512]{0:T(512)S(1)} %add_rsqrt_fusion), kind=kOutput, calls=%fused_computation.2 | convolution fusion | flops 6449266688 | bytes 22022144 | tf_op jit(solution)/shard_map/dot_general | solution.py:61
  80.8 0.0 reduce-scatter.2.cloned.1.call-update
  80.9 108.5 %reduce-scatter.2.cloned.1.call-done = bf16[1536,512]{0,1:T(8,128)(2,1)} async-done(((bf16[6144,512]{0,1:T(8,128)(2,1)}), bf16[1536,512]{0,1:T(8,128)(2,1)}) %reduce-scatter.2.cloned.1.call-update) | async-done | bytes 1572880 | tf_op jit(solution)/shard_map/reduce_scatter | solution.py:60
  (20 shorter events, 0.4 us)
Async XLA Ops:
  6.5 2.5 %copy-start = (bf16[512,1024]{1,0:T(8,128)(2,1)S(1)}, bf16[512,1024]{1,0:T(8,128)(2,1)}, u32[]{:S(2)}) copy-start(bf16[512,1024]{1,0:T(8,128)(2,1)} %param.7) | copy-start | bytes 3145732
  6.5 182.8 %reduce-scatter.2.cloned.1.call-start = ((), (), s32[]{:S(2)}) async-start(), calls=%async_computation.1 | async-start | bytes 7864320 | tf_op jit(solution)/shard_map/reduce_scatter | solution.py:60
  9.9 7.5 %collective-permute-start = (bf16[1,8,128,128]{3,2,1,0:T(8,128)(2,1)S(1)}, bf16[1,8,128,128]{3,2,1,0:T(8,128)(2,1)S(1)}, u32[]{:S(2)}, u32[]{:S(2)}) collective-permute-start(bf16[1,8,128,128]{3,2,1,0:T(8,128)(2,1)S(1)} %convert_bitcast_fusion), channel_id=1, source_target_pairs={{0,4},{4,8},{8,12},{12,16},{16,20},{20,24},{24,28},{28,0},{1,5},{5... | collective-permute-start | bytes 786440 | tf_op jit(solution)/shard_map/ppermute | solution.py:16
  17.4 7.8 %collective-permute-start.1 = (bf16[1,8,128,128]{3,2,1,0:T(8,128)(2,1)S(1)}, bf16[1,8,128,128]{3,2,1,0:T(8,128)(2,1)S(1)}, u32[]{:S(2)}, u32[]{:S(2)}) collective-permute-start(bf16[1,8,128,128]{3,2,1,0:T(8,128)(2,1)S(1)} %collective-permute-done), channel_id=1, source_target_pairs={{0,4},{4,8},{8,12},{12,16},{16,20},{20,24},{24,28},{28,0},{1,5},{5... | collective-permute-start | bytes 786440 | tf_op jit(solution)/shard_map/ppermute | solution.py:16
  17.4 7.9 %collective-permute-start.4 = (bf16[1,8,128,128]{3,2,1,0:T(8,128)(2,1)S(1)}, bf16[1,8,128,128]{3,2,1,0:T(8,128)(2,1)S(1)}, u32[]{:S(2)}, u32[]{:S(2)}) collective-permute-start(bf16[1,8,128,128]{3,2,1,0:T(8,128)(2,1)S(1)} %convert_bitcast_fusion), channel_id=1, source_target_pairs={{0,28},{4,0},{8,4},{12,8},{16,12},{20,16},{24,20},{28,24},{1,29},{... | collective-permute-start | bytes 786440 | tf_op jit(solution)/shard_map/ppermute | solution.py:18
  25.2 8.5 %collective-permute-start.2 = (bf16[1,8,128,128]{3,2,1,0:T(8,128)(2,1)S(1)}, bf16[1,8,128,128]{3,2,1,0:T(8,128)(2,1)}, u32[]{:S(2)}, u32[]{:S(2)}) collective-permute-start(bf16[1,8,128,128]{3,2,1,0:T(8,128)(2,1)S(1)} %collective-permute-done.1), channel_id=1, source_target_pairs={{0,4},{4,8},{8,12},{12,16},{16,20},{20,24},{24,28},{28,0},{1,5},{5... | collective-permute-start | bytes 786440 | tf_op jit(solution)/shard_map/ppermute | solution.py:16
  25.3 14.0 %collective-permute-start.5 = (bf16[1,8,128,128]{3,2,1,0:T(8,128)(2,1)S(1)}, bf16[1,8,128,128]{3,2,1,0:T(8,128)(2,1)}, u32[]{:S(2)}, u32[]{:S(2)}) collective-permute-start(bf16[1,8,128,128]{3,2,1,0:T(8,128)(2,1)S(1)} %collective-permute-done.4), channel_id=1, source_target_pairs={{0,28},{4,0},{8,4},{12,8},{16,12},{20,16},{24,20},{28,24},{1,29},{... | collective-permute-start | bytes 786440 | tf_op jit(solution)/shard_map/ppermute | solution.py:18
  33.7 8.3 %collective-permute-start.3 = (bf16[1,8,128,128]{3,2,1,0:T(8,128)(2,1)}, bf16[1,8,128,128]{3,2,1,0:T(8,128)(2,1)}, u32[]{:S(2)}, u32[]{:S(2)}) collective-permute-start(bf16[1,8,128,128]{3,2,1,0:T(8,128)(2,1)} %collective-permute-done.2), channel_id=1, source_target_pairs={{0,4},{4,8},{8,12},{12,16},{16,20},{20,24},{24,28},{28,0},{1,5},{5... | collective-permute-start | bytes 786440 | tf_op jit(solution)/shard_map/ppermute | solution.py:16
  39.3 6.9 %collective-permute-start.6 = (bf16[1,8,128,128]{3,2,1,0:T(8,128)(2,1)}, bf16[1,8,128,128]{3,2,1,0:T(8,128)(2,1)S(1)}, u32[]{:S(2)}, u32[]{:S(2)}) collective-permute-start(bf16[1,8,128,128]{3,2,1,0:T(8,128)(2,1)} %collective-permute-done.5), channel_id=1, source_target_pairs={{0,28},{4,0},{8,4},{12,8},{16,12},{20,16},{24,20},{28,24},{1,29},{... | collective-permute-start | bytes 786440 | tf_op jit(solution)/shard_map/ppermute | solution.py:18
  44.2 5.8 %copy-start.1 = (bf16[512,1024]{1,0:T(8,128)(2,1)S(1)}, bf16[512,1024]{1,0:T(8,128)(2,1)}, u32[]{:S(2)}) copy-start(bf16[512,1024]{1,0:T(8,128)(2,1)} %param.5) | copy-start | bytes 3145732
  44.2 5.8 %copy-start.2 = (f32[8,128,512]{2,1,0:T(8,128)S(1)}, f32[8,128,512]{2,1,0:T(8,128)}, u32[]{:S(2)}) copy-start(f32[8,128,512]{2,1,0:T(8,128)} %fusion.1) | copy-start | bytes 6291460
Sparse Core Ops, SparseCore 0:
  81.0 108.2 reduce-scatter.1
